TPU v7x, 256 devices: a whole 4x4x8 slice. The times are simulated.
256 devices in a mesh: gx: 8 (over y, core), gy: 16 (over x_lo, z), src: 2 (over x_hi).
Axes of the slice: x: 4 (x_hi: 2, x_lo: 2; x = x_hi * 2 + x_lo), y: 4, z: 8, core: 2. Of those that a mesh axis runs over, the one named last changes fastest.
Arguments:
- conductivity: float32 [16, 128, 128], P('gx', 'gy'), may hold values from 0.3 to 3
- electrodes: int32 [128, 2], replicated, may hold values from 0 to 262143
- pair_order: int32 [128], P('src'), may hold values from 0 to 127, each once
- initial_fields: float32 [128, 16, 128, 128], P('src', 'gx', 'gy'), as said below
- adjoint_fields: float32 [128, 16, 128, 128], P('src', 'gx', 'gy'), may hold values from -6 to 6
Outputs:
- potentials: float32 [128, 16, 128, 128], P('src', 'gx', 'gy')
- gradient: float32 [16, 128, 128], P('gx', 'gy', 'src')
Inputs may be any that keep to these rules, and one draw needn't show every extreme that they name: `electrodes`: flat cell index (x * 128 + y) * 128 + z. `pair_order`: each pair appears once. `initial_fields`: every entry lies within 6 / sqrt(262144) in magnitude.
All inputs are finite; a program needn't handle non-finite values.
Results may differ from a plain program's by a relative error of at most 0.00029.
Values sent between devices are 32-bit elements; how exact they have to be, the bound alone decides.
No kernel may reach another device: no remote copies, remote signals or barrier semaphores. Data moves between devices by JAX's collectives and lax.ppermute only.
A program may use at most 64 MiB of HBM per device.

v0:
```python
import jax
import jax.numpy as jnp
from jax import lax
from jax.sharding import PartitionSpec as P

ITERS = 2
INJECT = 4.0


def padded_2(block, sides, width):
    for axis, dim in sides:
        count = lax.axis_size(axis)
        forward = [(i, i + 1) for i in range(count - 1)]
        backward = [(target, source) for source, target in forward]
        low = lax.ppermute(
            lax.slice_in_dim(block, block.shape[dim] - width, None, axis=dim), axis, forward
        )
        high = lax.ppermute(lax.slice_in_dim(block, 0, width, axis=dim), axis, backward)
        block = jnp.concatenate([low, block, high], axis=dim)
    return block


def conductances(sig_pad):
    full = jnp.pad(sig_pad, ((0, 0), (0, 0), (1, 1)))
    cond_x = 0.5 * (full[1:, 1:-1, 1:-1] + full[:-1, 1:-1, 1:-1])
    cond_y = 0.5 * (full[1:-1, 1:, 1:-1] + full[1:-1, :-1, 1:-1])
    cond_z = 0.5 * (full[1:-1, 1:-1, 1:] + full[1:-1, 1:-1, :-1])
    return (cond_x, cond_y, cond_z)


def operator(padded, conds):
    full = jnp.pad(padded, ((0, 0), (0, 0), (0, 0), (1, 1)))
    flux_x = conds[0] * (full[:, 1:, 1:-1, 1:-1] - full[:, :-1, 1:-1, 1:-1])
    flux_y = conds[1] * (full[:, 1:-1, 1:, 1:-1] - full[:, 1:-1, :-1, 1:-1])
    flux_z = conds[2] * (full[:, 1:-1, 1:-1, 1:] - full[:, 1:-1, 1:-1, :-1])
    return (
        flux_x[:, :-1]
        - flux_x[:, 1:]
        + (flux_y[:, :, :-1] - flux_y[:, :, 1:])
        + (flux_z[..., :-1] - flux_z[..., 1:])
    )


def gram_of(left, right):
    return jnp.einsum("axyz,bxyz->ab", left, right, precision=lax.Precision.HIGHEST)


def combine_cols(field, matrix):
    return jnp.einsum("axyz,ab->bxyz", field, matrix, precision=lax.Precision.HIGHEST)


def posdef_solve(matrix, right):
    lower = jnp.linalg.cholesky(matrix)
    middle = lax.linalg.triangular_solve(lower, right, left_side=True, lower=True)
    return lax.linalg.triangular_solve(lower, middle, left_side=True, lower=True, transpose_a=True)


def one_hot(cells, start, count):
    return (cells[:, None] == start + jnp.arange(count, dtype=jnp.int32)[None, :]).astype(
        jnp.float32
    )


def face_terms(field_pad, adjoint_pad):
    fu = jnp.pad(field_pad, ((0, 0), (0, 0), (0, 0), (1, 1)))
    fl = jnp.pad(adjoint_pad, ((0, 0), (0, 0), (0, 0), (1, 1)))
    term_x = jnp.sum(
        (fu[:, 1:, 1:-1, 1:-1] - fu[:, :-1, 1:-1, 1:-1])
        * (fl[:, 1:, 1:-1, 1:-1] - fl[:, :-1, 1:-1, 1:-1]),
        axis=0,
    )
    term_y = jnp.sum(
        (fu[:, 1:-1, 1:, 1:-1] - fu[:, 1:-1, :-1, 1:-1])
        * (fl[:, 1:-1, 1:, 1:-1] - fl[:, 1:-1, :-1, 1:-1]),
        axis=0,
    )
    term_z = jnp.sum(
        (fu[:, 1:-1, 1:-1, 1:] - fu[:, 1:-1, 1:-1, :-1])
        * (fl[:, 1:-1, 1:-1, 1:] - fl[:, 1:-1, 1:-1, :-1]),
        axis=0,
    )
    return (term_x, term_y, term_z)


def on_device(conductivity, electrodes, pair_order, initial_fields, adjoint_fields):
    cells_x, cells_y, cells_z = conductivity.shape
    columns = initial_fields.shape[0]
    total_y = lax.axis_size("gy") * cells_y
    start_x = lax.axis_index("gx") * cells_x
    start_y = lax.axis_index("gy") * cells_y
    picked = jnp.take(electrodes, pair_order, axis=0)

    def point_source(flat):
        xs = flat // (total_y * cells_z)
        ys = flat // cells_z % total_y
        zs = flat % cells_z
        return jnp.einsum(
            "cx,cy,cz->cxyz",
            one_hot(xs, start_x, cells_x),
            one_hot(ys, start_y, cells_y),
            one_hot(zs, 0, cells_z),
        )

    right = INJECT * (point_source(picked[:, 0]) - point_source(picked[:, 1]))
    stacked = jnp.concatenate([conductivity[None], initial_fields], axis=0)
    padded = padded_2(stacked, (("gx", 1), ("gy", 2)), 1)
    conds = conductances(padded[0])
    iterate = initial_fields
    iter_pad = padded[1:]
    residual = right - operator(iter_pad, conds)
    direction = residual
    res_gram = lax.psum(gram_of(residual, residual), ("gx", "gy"))
    for iteration in range(ITERS):
        dir_pad = padded_2(direction, (("gx", 1), ("gy", 2)), 1)
        image = operator(dir_pad, conds)
        curv_gram = lax.psum(gram_of(direction, image), ("gx", "gy"))
        step_mat = posdef_solve(curv_gram, res_gram)
        iterate = iterate + combine_cols(direction, step_mat)
        residual = residual - combine_cols(image, step_mat)
        if iteration + 1 < ITERS:
            new_gram = lax.psum(gram_of(residual, residual), ("gx", "gy"))
            turn_mat = posdef_solve(res_gram, new_gram)
            direction = residual + combine_cols(direction, turn_mat)
            res_gram = new_gram
    both = jnp.concatenate([iterate, adjoint_fields], axis=0)
    both_pad = padded_2(both, (("gx", 1), ("gy", 2)), 1)
    term_x, term_y, term_z = face_terms(both_pad[:columns], both_pad[columns:])
    local_grad = (
        -0.5
        / columns
        * (
            term_x[:-1]
            + term_x[1:]
            + term_y[:, :-1]
            + term_y[:, 1:]
            + term_z[..., :-1]
            + term_z[..., 1:]
        )
    )
    share = cells_z // lax.axis_size("src")
    summed = lax.psum(local_grad, "src")
    gradient = lax.dynamic_slice_in_dim(summed, lax.axis_index("src") * share, share, 2)
    return (iterate, gradient)


def solution(mesh):
    placed = (
        P("gx", "gy", None),
        P(),
        P("src"),
        P("src", "gx", "gy", None),
        P("src", "gx", "gy", None),
    )
    return jax.shard_map(
        on_device,
        mesh=mesh,
        in_specs=placed,
        out_specs=(P("src", "gx", "gy", None), P("gx", "gy", "src")),
        check_vma=False,
    )
```

profile of v0, /device:TPU:40, one launch (start us, length us, event | category | flops | bytes accessed | tf_op | source)
XLA Modules:
  0.0 1785.7 jit_solution(18146952785579994291)
XLA Ops:
  4.5 3.6 collective-permute-start.1
  12.4 3.8 collective-permute-start.2
  20.2 3.9 collective-permute-done.3
  32.0 3.8 collective-permute-done.5
  37.9 4.8 collective-permute-start.7
  47.5 485.9 %all-reduce.6 = (f32[64,64]{0,1:T(8,128)S(1)}, f32[64,64]{0,1:T(8,128)S(1)}) all-reduce(f32[64,64]{0,1:T(8,128)S(1)} %convolution_bitcast_fusion.5, f32[64,64]{0,1:T(8,128)S(1)} %convolution_bitcast_fusion.6), channel_id=1, replica_groups=mesh['gx'=8,'gy'=16,'src'=2] {'gx','gy'}, use_global_device_ids=true, to_apply=%region_3.5 | all-reduce | flops 8192 | bytes 65536 | tf_op jit(solution)/shard_map/psum | solution.py:112
  533.5 5.8 cholesky.70
  540.7 4.9 custom-call.15
  545.7 5.8 cholesky.59
  552.9 4.9 custom-call.13
  559.4 550.9 %psum.37 = f32[64,64]{1,0:T(8,128)S(1)} all-reduce(f32[64,64]{1,0:T(8,128)S(1)} %convolution_bitcast_fusion.3), channel_id=1, replica_groups=mesh['gx'=8,'gy'=16,'src'=2] {'gx','gy'}, use_global_device_ids=true, to_apply=%region_4.8 | all-reduce | flops 4096 | bytes 32768 | tf_op jit(solution)/shard_map/psum | solution.py:121
  1111.4 38.1 %collective-permute-start.8 = (f32[64,1,8,128]{3,0,2,1:T(8,128)S(1)}, f32[64,1,8,128]{3,0,2,1:T(8,128)S(1)}, u32[]{:S(2)}, u32[]{:S(2)}) collective-permute-start(f32[64,1,8,128]{3,0,2,1:T(8,128)S(1)} %get-tuple-element.39), channel_id=1, source_target_pairs={{32,0},{64,32},{96,64},{128,96},{160,128},{192,160},{224,192},{33,... | collective-permute-start | bytes 786440 | tf_op jit(solution)/shard_map/ppermute | solution.py:18
  1153.4 27.1 %collective-permute-done.9 = f32[64,1,8,128]{3,0,2,1:T(8,128)S(1)} collective-permute-done((f32[64,1,8,128]{3,0,2,1:T(8,128)S(1)}, f32[64,1,8,128]{3,0,2,1:T(8,128)S(1)}, u32[]{:S(2)}, u32[]{:S(2)}) %collective-permute-start.9) | collective-permute-done | bytes 262176 | tf_op jit(solution)/shard_map/ppermute | solution.py:15
  1180.5 5.1 collective-permute-start.10
  1188.1 4.4 collective-permute-done.11
  1194.4 481.9 %psum.38 = f32[64,64]{0,1:T(8,128)S(1)} all-reduce(f32[64,64]{0,1:T(8,128)S(1)} %convolution_bitcast_fusion.1), channel_id=1, replica_groups=mesh['gx'=8,'gy'=16,'src'=2] {'gx','gy'}, use_global_device_ids=true, to_apply=%region_5.9 | all-reduce | flops 4096 | bytes 32768 | tf_op jit(solution)/shard_map/psum | solution.py:116
  1676.4 5.8 cholesky.81
  1683.6 4.9 custom-call.17
  1689.7 37.9 %collective-permute-start.12 = (f32[128,1,8,128]{3,0,2,1:T(8,128)S(1)}, f32[128,1,8,128]{3,0,2,1:T(8,128)S(1)}, u32[]{:S(2)}, u32[]{:S(2)}) collective-permute-start(f32[128,1,8,128]{3,0,2,1:T(8,128)S(1)} %get-tuple-element.31), channel_id=1, source_target_pairs={{32,0},{64,32},{96,64},{128,96},{160,128},{192,160},{224,192},{33,... | collective-permute-start | bytes 1572872 | tf_op jit(solution)/shard_map/ppermute | solution.py:18
  1730.6 3.6 collective-permute-done.12
  1734.2 27.1 %collective-permute-done.13 = f32[128,1,8,128]{3,0,2,1:T(8,128)S(1)} collective-permute-done((f32[128,1,8,128]{3,0,2,1:T(8,128)S(1)}, f32[128,1,8,128]{3,0,2,1:T(8,128)S(1)}, u32[]{:S(2)}, u32[]{:S(2)}) %collective-permute-start.13) | collective-permute-done | bytes 524320 | tf_op jit(solution)/shard_map/ppermute | solution.py:15
  1761.4 7.5 collective-permute-start.14
  1772.7 4.4 collective-permute-done.15
  1778.6 6.5 psum.39
  (108 shorter events, 51.9 us)
Async XLA Ops:
  0.6 11.8 copy-start.2
  2.6 9.0 collective-permute-start
  4.5 7.9 collective-permute-start.1
  12.4 7.7 collective-permute-start.2
  16.3 7.8 collective-permute-start.3
  25.6 5.0 copy-start.1
  26.2 5.8 collective-permute-start.4
  28.1 7.7 collective-permute-start.5
  35.8 8.5 collective-permute-start.6
  37.9 7.6 collective-permute-start.7
  558.3 593.2 %copy-start = (f32[64,2,8,128]{3,2,1,0:T(8,128)S(1)}, f32[64,2,8,128]{3,2,1,0:T(8,128)}, u32[]{:S(2)}) copy-start(f32[64,2,8,128]{3,2,1,0:T(8,128)} %param.13) | copy-start | bytes 1572868
  1111.4 42.0 %collective-permute-start.8 = (f32[64,1,8,128]{3,0,2,1:T(8,128)S(1)}, f32[64,1,8,128]{3,0,2,1:T(8,128)S(1)}, u32[]{:S(2)}, u32[]{:S(2)}) collective-permute-start(f32[64,1,8,128]{3,0,2,1:T(8,128)S(1)} %get-tuple-element.39), channel_id=1, source_target_pairs={{32,0},{64,32},{96,64},{128,96},{160,128},{192,160},{224,192},{33,... | collective-permute-start | bytes 786440 | tf_op jit(solution)/shard_map/ppermute | solution.py:18
  1149.5 31.0 %collective-permute-start.9 = (f32[64,1,8,128]{3,0,2,1:T(8,128)S(1)}, f32[64,1,8,128]{3,0,2,1:T(8,128)S(1)}, u32[]{:S(2)}, u32[]{:S(2)}) collective-permute-start(f32[64,1,8,128]{3,0,2,1:T(8,128)S(1)} %get-tuple-element.38), channel_id=1, source_target_pairs={{0,32},{32,64},{64,96},{96,128},{128,160},{160,192},{192,224},{1,3... | collective-permute-start | bytes 786440 | tf_op jit(solution)/shard_map/ppermute | solution.py:15
  1180.5 7.6 collective-permute-start.10
  1185.6 6.9 collective-permute-start.11
  1689.7 44.6 %collective-permute-start.12 = (f32[128,1,8,128]{3,0,2,1:T(8,128)S(1)}, f32[128,1,8,128]{3,0,2,1:T(8,128)S(1)}, u32[]{:S(2)}, u32[]{:S(2)}) collective-permute-start(f32[128,1,8,128]{3,0,2,1:T(8,128)S(1)} %get-tuple-element.31), channel_id=1, source_target_pairs={{32,0},{64,32},{96,64},{128,96},{160,128},{192,160},{224,192},{33,... | collective-permute-start | bytes 1572872 | tf_op jit(solution)/shard_map/ppermute | solution.py:18
  1727.5 33.8 %collective-permute-start.13 = (f32[128,1,8,128]{3,0,2,1:T(8,128)S(1)}, f32[128,1,8,128]{3,0,2,1:T(8,128)S(1)}, u32[]{:S(2)}, u32[]{:S(2)}) collective-permute-start(f32[128,1,8,128]{3,0,2,1:T(8,128)S(1)} %get-tuple-element.30), channel_id=1, source_target_pairs={{0,32},{32,64},{64,96},{96,128},{128,160},{160,192},{192,224},{1,3... | collective-permute-start | bytes 1572872 | tf_op jit(solution)/shard_map/ppermute | solution.py:15
  1761.4 11.3 collective-permute-start.14
  1768.8 8.3 collective-permute-start.15
where the time goes:
time: 1790 us
  blocking collectives  1530 us (85%)
  starting transfers between devices  119 us (7%)
  waiting for transfers between devices  83.3 us (5%)
  other arithmetic  45.7 us (3%)
    psum x1, blocking collectives, on_device(): new_gram = lax.psum(gram_of(residual, residual), ('gx', 'gy'))  551 us
    psum x1, blocking collectives, on_device(): res_gram = lax.psum(gram_of(residual, residual), ('gx', 'gy'))  486 us
    psum x1, blocking collectives, on_device(): curv_gram = lax.psum(gram_of(direction, image), ('gx', 'gy'))  482 us
    ppermute x8, starting transfers between devices, padded_2(): lax.ppermute(lax.slice_in_dim(block, 0, width, axis=dim), axis, backward)  98.1 us
    ppermute x8, waiting for transfers between devices, padded_2(): lax.ppermute(lax.slice_in_dim(block, block.shape[dim] - width, None, axis...  69.9 us
  transfers between devices with their start and end apart: 16, of which 15 were waited for; matrix products, arithmetic and copies ran while one was open for 0% of the time, Pallas kernels for 0%

commit v1 on v0

--- a/solution.py
+++ b/solution.py
@@ -2,9 +2,15 @@
 import jax.numpy as jnp
 from jax import lax
 from jax.sharding import PartitionSpec as P
+from jax.lax import all_gather
 
 ITERS = 2
 INJECT = 4.0
+
+
+def shape_the_columns(panel, along_axis):
+    mid_arr = all_gather(panel, along_axis).sum(axis=0)
+    return mid_arr
 
 
 def padded_2(block, sides, width):
@@ -118,7 +124,7 @@
         iterate = iterate + combine_cols(direction, step_mat)
         residual = residual - combine_cols(image, step_mat)
         if iteration + 1 < ITERS:
-            new_gram = lax.psum(gram_of(residual, residual), ("gx", "gy"))
+            new_gram = shape_the_columns(gram_of(residual, residual), ("gx", "gy"))
             turn_mat = posdef_solve(res_gram, new_gram)
             direction = residual + combine_cols(direction, turn_mat)
             res_gram = new_gram

time: 1790 us -> 1600 us (0.89)
  blocking collectives: 1530 us -> 974 us
  waiting for transfers between devices: 83.3 us -> 453 us
  starting transfers between devices: 119 us -> 99.3 us
    psum x1 -> x0, blocking collectives: 551 us -> none  [on_device(): new_gram = lax.psum(gram_of(residual, residual), ('gx', 'gy'))]
    all_gather x0 -> x1, waiting for transfers between devices: none -> 395 us  [shape_the_columns(): mid_arr = all_gather(panel, along_axis).sum(axis=0)]
    ppermute x8, waiting for transfers between devices: 69.9 us -> 43.7 us  [padded_2(): lax.ppermute(lax.slice_in_dim(block, block.shape[dim] - width, None, axis...]
    ppermute x8, starting transfers between devices: 98.1 us -> 75.1 us  [padded_2(): lax.ppermute(lax.slice_in_dim(block, 0, width, axis=dim), axis, backward)]
  transfers between devices with their start and end apart: 16 -> 17, of which waited for: 15 -> 16; matrix products, arithmetic and copies ran while one was open for 0% -> 1% of each run, Pallas kernels for 0% -> 0%
where the time goes in v1:
time: 1600 us
  blocking collectives  974 us (61%)
  waiting for transfers between devices  453 us (28%)
  starting transfers between devices  99.3 us (6%)
  other arithmetic  48.3 us (3%)
    psum x1, blocking collectives, on_device(): res_gram = lax.psum(gram_of(residual, residual), ('gx', 'gy'))  486 us
    psum x1, blocking collectives, on_device(): curv_gram = lax.psum(gram_of(direction, image), ('gx', 'gy'))  481 us
    all_gather x1, waiting for transfers between devices, shape_the_columns(): mid_arr = all_gather(panel, along_axis).sum(axis=0)  395 us
    ppermute x8, starting transfers between devices, padded_2(): lax.ppermute(lax.slice_in_dim(block, 0, width, axis=dim), axis, backward)  75.1 us
    ppermute x8, waiting for transfers between devices, padded_2(): lax.ppermute(lax.slice_in_dim(block, block.shape[dim] - width, None, axis...  43.7 us
  transfers between devices with their start and end apart: 17, of which 16 were waited for; matrix products, arithmetic and copies ran while one was open for 1% of the time, Pallas kernels for 0%

profile of v1, /device:TPU:40, one launch (start us, length us, event | category | flops | bytes accessed | tf_op | source)
XLA Modules:
  0.0 1601.0 jit_solution(7764617981133681311)
XLA Ops:
  11.1 3.6 collective-permute-start.1
  19.0 3.8 collective-permute-start.2
  26.8 3.9 collective-permute-done.3
  38.6 3.8 collective-permute-done.5
  44.4 4.8 collective-permute-start.7
  54.1 486.1 %all-reduce.6 = (f32[64,64]{0,1:T(8,128)S(1)}, f32[64,64]{0,1:T(8,128)S(1)}) all-reduce(f32[64,64]{0,1:T(8,128)S(1)} %convolution_bitcast_fusion.5, f32[64,64]{0,1:T(8,128)S(1)} %convolution_bitcast_fusion.6), channel_id=1, replica_groups=mesh['gx'=8,'gy'=16,'src'=2] {'gx','gy'}, use_global_device_ids=true, to_apply=%region_3.5 | all-reduce | flops 8192 | bytes 65536 | tf_op jit(solution)/shard_map/psum | solution.py:118
  540.2 5.8 cholesky.59
  547.4 4.9 custom-call.13
  554.9 5.8 cholesky.70
  562.1 4.9 custom-call.15
  567.0 395.3 %all-gather.3.cloned.1.call-done = f32[8192,64]{1,0:T(8,128)} async-done(((f32[64,64]{1,0:T(8,128)}), f32[8192,64]{1,0:T(8,128)}) %all-gather.3.cloned.1.call-update) | async-done | bytes 2097168 | tf_op jit(solution)/shard_map/all_gather | solution.py:12
  962.2 2.6 reduce_sum.36
  965.9 18.6 %collective-permute-start.8 = (f32[64,1,8,128]{3,0,2,1:T(8,128)S(1)}, f32[64,1,8,128]{3,0,2,1:T(8,128)S(1)}, u32[]{:S(2)}, u32[]{:S(2)}) collective-permute-start(f32[64,1,8,128]{3,0,2,1:T(8,128)S(1)} %get-tuple-element.39), channel_id=1, source_target_pairs={{32,0},{64,32},{96,64},{128,96},{160,128},{192,160},{224,192},{33,... | collective-permute-start | bytes 786440 | tf_op jit(solution)/shard_map/ppermute | solution.py:24
  988.5 3.8 collective-permute-done.9
  994.2 5.4 collective-permute-start.11
  1004.0 481.1 %psum.30 = f32[64,64]{0,1:T(8,128)S(1)} all-reduce(f32[64,64]{0,1:T(8,128)S(1)} %convolution_bitcast_fusion.1), channel_id=1, replica_groups=mesh['gx'=8,'gy'=16,'src'=2] {'gx','gy'}, use_global_device_ids=true, to_apply=%region_5.9 | all-reduce | flops 4096 | bytes 32768 | tf_op jit(solution)/shard_map/psum | solution.py:122
  1485.2 5.8 cholesky.81
  1492.4 4.9 custom-call.17
  1498.5 37.9 %collective-permute-start.12 = (f32[128,1,8,128]{3,0,2,1:T(8,128)S(1)}, f32[128,1,8,128]{3,0,2,1:T(8,128)S(1)}, u32[]{:S(2)}, u32[]{:S(2)}) collective-permute-start(f32[128,1,8,128]{3,0,2,1:T(8,128)S(1)} %get-tuple-element.31), channel_id=1, source_target_pairs={{32,0},{64,32},{96,64},{128,96},{160,128},{192,160},{224,192},{33,... | collective-permute-start | bytes 1572872 | tf_op jit(solution)/shard_map/ppermute | solution.py:24
  1539.4 3.6 collective-permute-done.12
  1543.1 27.1 %collective-permute-done.13 = f32[128,1,8,128]{3,0,2,1:T(8,128)S(1)} collective-permute-done((f32[128,1,8,128]{3,0,2,1:T(8,128)S(1)}, f32[128,1,8,128]{3,0,2,1:T(8,128)S(1)}, u32[]{:S(2)}, u32[]{:S(2)}) %collective-permute-start.13) | collective-permute-done | bytes 524320 | tf_op jit(solution)/shard_map/ppermute | solution.py:21
  1570.2 7.0 collective-permute-start.14
  1581.1 4.4 collective-permute-done.15
  1587.0 6.5 psum.31
  (111 shorter events, 54.7 us)
Async XLA Ops:
  7.2 11.8 copy-start.2
  7.2 955.1 %all-gather.3.cloned.1.call-start = ((), (), s32[]{:S(2)}) async-start(), calls=%async_computation | async-start | bytes 4227072 | tf_op jit(solution)/shard_map/all_gather | solution.py:12
  9.2 9.0 collective-permute-start
  11.1 7.9 collective-permute-start.1
  19.0 7.7 collective-permute-start.2
  22.9 7.8 collective-permute-start.3
  32.8 5.8 collective-permute-start.4
  34.7 7.7 collective-permute-start.5
  42.4 8.5 collective-permute-start.6
  44.4 7.6 collective-permute-start.7
  53.5 501.1 %copy-start.1 = (f32[64,2,8,128]{3,2,1,0:T(8,128)S(1)}, f32[64,2,8,128]{3,2,1,0:T(8,128)}, u32[]{:S(2)}) copy-start(f32[64,2,8,128]{3,2,1,0:T(8,128)} %param.14) | copy-start | bytes 1572868
  962.2 24.3 %copy-start = (f32[64,2,8,128]{3,2,1,0:T(8,128)S(1)}, f32[64,2,8,128]{3,2,1,0:T(8,128)}, u32[]{:S(2)}) copy-start(f32[64,2,8,128]{3,2,1,0:T(8,128)} %param.13) | copy-start | bytes 1572868
  965.9 22.5 %collective-permute-start.8 = (f32[64,1,8,128]{3,0,2,1:T(8,128)S(1)}, f32[64,1,8,128]{3,0,2,1:T(8,128)S(1)}, u32[]{:S(2)}, u32[]{:S(2)}) collective-permute-start(f32[64,1,8,128]{3,0,2,1:T(8,128)S(1)} %get-tuple-element.39), channel_id=1, source_target_pairs={{32,0},{64,32},{96,64},{128,96},{160,128},{192,160},{224,192},{33,... | collective-permute-start | bytes 786440 | tf_op jit(solution)/shard_map/ppermute | solution.py:24
  984.6 7.7 collective-permute-start.9
  992.3 8.3 collective-permute-start.10
  994.2 7.9 collective-permute-start.11
  1498.5 44.5 %collective-permute-start.12 = (f32[128,1,8,128]{3,0,2,1:T(8,128)S(1)}, f32[128,1,8,128]{3,0,2,1:T(8,128)S(1)}, u32[]{:S(2)}, u32[]{:S(2)}) collective-permute-start(f32[128,1,8,128]{3,0,2,1:T(8,128)S(1)} %get-tuple-element.31), channel_id=1, source_target_pairs={{32,0},{64,32},{96,64},{128,96},{160,128},{192,160},{224,192},{33,... | collective-permute-start | bytes 1572872 | tf_op jit(solution)/shard_map/ppermute | solution.py:24
  1536.4 33.8 %collective-permute-start.13 = (f32[128,1,8,128]{3,0,2,1:T(8,128)S(1)}, f32[128,1,8,128]{3,0,2,1:T(8,128)S(1)}, u32[]{:S(2)}, u32[]{:S(2)}) collective-permute-start(f32[128,1,8,128]{3,0,2,1:T(8,128)S(1)} %get-tuple-element.30), channel_id=1, source_target_pairs={{0,32},{32,64},{64,96},{96,128},{128,160},{160,192},{192,224},{1,3... | collective-permute-start | bytes 1572872 | tf_op jit(solution)/shard_map/ppermute | solution.py:21
  1570.2 10.9 collective-permute-start.14
  1577.2 8.3 collective-permute-start.15
Sparse Core Ops, SparseCore 0:
  554.7 407.4 all-gather.2
